TPU v7x, 128 devices: a whole 4x4x4 slice. The times are simulated.
128 devices in a mesh: row: 8 (over y, core), col: 16 (over z, x).
Axes of the slice: x: 4, y: 4, z: 4, core: 2. Of those that a mesh axis runs over, the one named last changes fastest.
Arguments:
- fock: bfloat16 [32768, 16, 2048], P('row', 'col'), may hold values from -6 to 6
- lmo_coef: bfloat16 [32768, 1024], P(('row', 'col')), may hold values from -0.078125 to 0.078125
- three_index: bfloat16 [32768, 512], P(('row', 'col')), may hold values from -6 to 6
- rotation: bfloat16 [16, 8, 1024, 512], P('col', 'row'), may hold values from -0.1875 to 0.1875
- lmo_ids: int32 [16, 8], replicated, may hold values from 0 to 127, as said below
- domains: int32 [128, 8], replicated, may hold values from -1 to 255, as said below
Outputs:
- proj_fock: float32 [16, 8, 512, 512], P('col', 'row')
- three_rot: bfloat16 [16, 8, 512, 512], P('col', 'row')
Inputs may be any that keep to these rules, and one draw needn't show every extreme that they name: `lmo_ids`: every LMO number appears exactly once; row o lists the 8 LMOs owned by column set o. `domains`: entry k of a list is -1 or a block of row panel k; entry 0 is never -1. The present blocks of one list lie in distinct column sets. For one owner o and one entry k, the blocks of the lists of lmo_ids[o, j] over all j lie in distinct column sets; for one j and one entry k, those of lmo_ids[o, j] over all o do too.
All inputs are finite; a program needn't handle non-finite values.
Results may differ from a plain program's by a relative error of at most 0.02.
Values may be sent and summed in bfloat16 or wider, within the bound.
No kernel may reach another device: no remote copies, remote signals or barrier semaphores. Data moves between devices by JAX's collectives and lax.ppermute only.
A program may use at most 192 MiB of HBM per device.

v0:
```python
import jax
import jax.numpy as jnp
from jax import lax
from jax.sharding import PartitionSpec as P

BLK = 128
F32 = jnp.float32
BF16 = jnp.bfloat16


def pick(mask, table):
    return jnp.sum(jnp.where(mask, table, 0), axis=-1)


def body(fock, lmo_coef, three_index, rotation, lmo_ids, domains):
    num_sets = lax.axis_size("col")
    my_row = lax.axis_index("row")
    my_col = lax.axis_index("col")
    dev_rows = lmo_coef.shape[0]
    occ_width = lmo_coef.shape[1]
    dev_blocks = dev_rows // BLK
    dom_blocks = domains.shape[1]
    dom_width = dom_blocks * BLK
    panel_fock = fock[:, 0, :]
    panel_blocks = panel_fock.shape[0] // BLK
    col_blocks = panel_fock.shape[1] // BLK
    doms = jnp.take(domains, lmo_ids, axis=0)
    present = doms >= 0
    clipped = jnp.maximum(doms, 0)
    flat = clipped // dev_blocks
    cset = flat % num_sets
    sub = clipped % dev_blocks
    panel = flat // num_sets
    row_tile = cset * dev_blocks + sub
    col_tile = panel * dev_blocks + sub
    pres_k = lax.dynamic_index_in_dim(present, my_row, 2, keepdims=False)
    cset_k = lax.dynamic_index_in_dim(cset, my_row, 2, keepdims=False)
    sub_k = lax.dynamic_index_in_dim(sub, my_row, 2, keepdims=False)
    rtile_k = lax.dynamic_index_in_dim(row_tile, my_row, 2, keepdims=False)
    mine_k = pres_k & (cset_k == my_col)
    sub_range = jnp.arange(dev_blocks, dtype=jnp.int32)
    sel1 = jnp.any(mine_k[:, :, None] & (sub_k[:, :, None] == sub_range), axis=0).astype(BF16)
    mine2 = present & (cset == my_col)
    has2 = jnp.any(mine2, axis=0)
    rt = pick(
        mine2.transpose(1, 2, 0),
        jnp.broadcast_to(rtile_k.T[:, None, :], mine2.transpose(1, 2, 0).shape),
    )
    ok1 = jnp.any(mine2.transpose(1, 2, 0) & pres_k.T[:, None, :], axis=-1)
    ct = pick(mine2.transpose(1, 2, 0), col_tile.transpose(1, 2, 0))
    fock_tiles = panel_fock.reshape(panel_blocks, BLK, col_blocks, BLK)
    send1_fock = fock_tiles[rt, :, ct, :]
    send1_fock = jnp.where((has2 & ok1)[:, :, None, None], send1_fock, jnp.zeros_like(send1_fock))
    in_rows = jnp.concatenate([lmo_coef, three_index], axis=1).reshape(dev_blocks, BLK, -1)
    send1_rows = jnp.einsum("js,sbw->jbw", sel1, in_rows, preferred_element_type=F32).astype(BF16)
    recv1_rows, recv1_fock = (
        lax.all_to_all(send1_rows, "row", 0, 0, tiled=True),
        lax.all_to_all(send1_fock, "row", 0, 0, tiled=True),
    )
    pres_j = lax.dynamic_index_in_dim(present, my_row, 1, keepdims=False)
    cset_j = lax.dynamic_index_in_dim(cset, my_row, 1, keepdims=False)
    sel2 = (pres_j & (cset_j == my_col)).astype(BF16)
    send2_rows = jnp.einsum("ok,kbw->obw", sel2, recv1_rows, preferred_element_type=F32).astype(
        BF16
    )
    send2_fock = jnp.einsum("ok,akbt->oabt", sel2, recv1_fock, preferred_element_type=F32).astype(
        BF16
    )
    recv2_rows, recv2_fock = (
        lax.all_to_all(send2_rows, "col", 0, 0, tiled=True),
        lax.all_to_all(send2_fock, "col", 0, 0, tiled=True),
    )
    pres_o = lax.dynamic_index_in_dim(pres_j, my_col, 0, keepdims=False)
    cset_o = lax.dynamic_index_in_dim(cset_j, my_col, 0, keepdims=False)
    set_range = jnp.arange(num_sets, dtype=jnp.int32)
    sel3 = (pres_o[:, None] & (cset_o[:, None] == set_range)).astype(BF16)
    rows_dom = jnp.einsum("ks,sbw->kbw", sel3, recv2_rows, preferred_element_type=F32).astype(BF16)
    rows_dom = rows_dom.reshape(dom_width, -1)
    domain_fock = jnp.einsum("ks,sabt->abkt", sel3, recv2_fock, preferred_element_type=F32).astype(
        BF16
    )
    domain_fock = domain_fock.reshape(dom_width, dom_width)
    gathered = lax.all_gather(lmo_coef, "row", axis=0, tiled=True)
    coef_b = lax.psum_scatter(
        jnp.dot(panel_fock, gathered, preferred_element_type=F32).astype(BF16),
        "col",
        scatter_dimension=0,
        tiled=True,
    )
    occ_term = jnp.einsum("ri,rj->ij", lmo_coef, coef_b, preferred_element_type=F32)
    occ_part = lax.psum_scatter(occ_term, ("row", "col"), scatter_dimension=0, tiled=True)
    occ_b = lax.all_gather(occ_part.astype(BF16), ("row", "col"), axis=0, tiled=True)
    fc_blocks = coef_b.reshape(dev_blocks, BLK, occ_width)
    fc1 = jnp.einsum("js,sbw->jbw", sel1, fc_blocks, preferred_element_type=F32).astype(BF16)
    fc1 = lax.all_to_all(fc1, "row", 0, 0, tiled=True)
    fc2 = jnp.einsum("ok,kbw->obw", sel2, fc1, preferred_element_type=F32).astype(BF16)
    fc2 = lax.all_to_all(fc2, "col", 0, 0, tiled=True)
    fc_dom = jnp.einsum("ks,sbw->kbw", sel3, fc2, preferred_element_type=F32).reshape(
        dom_width, occ_width
    )
    coef_dom = rows_dom[:, :occ_width]
    three_dom = rows_dom[:, occ_width:]
    correction = jnp.dot(coef_dom, occ_b, preferred_element_type=F32)
    proj_dom = (fc_dom - 0.5 * correction).astype(BF16)
    slot_rot = rotation[0, 0]
    fock_half = jnp.dot(domain_fock, slot_rot, preferred_element_type=F32).astype(BF16)
    fock_rot = jnp.einsum("xm,xn->mn", slot_rot, fock_half, preferred_element_type=F32)
    coef_rot = jnp.einsum("xm,xi->mi", slot_rot, coef_dom, preferred_element_type=F32).astype(BF16)
    proj_rot = jnp.einsum("xm,xi->mi", slot_rot, proj_dom, preferred_element_type=F32).astype(BF16)
    proj_fock = fock_rot - jnp.einsum("mi,ni->mn", coef_rot, proj_rot, preferred_element_type=F32)
    proj_fock = proj_fock - jnp.einsum("mi,ni->mn", proj_rot, coef_rot, preferred_element_type=F32)
    three_rot = jnp.einsum("xm,xu->mu", slot_rot, three_dom, preferred_element_type=F32).astype(
        BF16
    )
    return (proj_fock[None, None], three_rot[None, None])


def solution(mesh):
    placed = (
        P("row", "col", None),
        P(("row", "col"), None),
        P(("row", "col"), None),
        P("col", "row", None, None),
        P(),
        P(),
    )
    return jax.shard_map(
        body,
        mesh=mesh,
        in_specs=placed,
        out_specs=(P("col", "row", None, None), P("col", "row", None, None)),
        check_vma=False,
    )
```

profile of v0, /device:TPU:1, one launch (start us, length us, event | category | flops | bytes accessed | tf_op | source)
XLA Modules:
  0.0 967.6 jit_solution(5314930313470861836)
XLA Ops:
  8.0 37.6 %all-gather.3.cloned.1.call-done = bf16[2048,1024]{1,0:T(8,128)(2,1)} async-done(((bf16[256,1024]{1,0:T(8,128)(2,1)}), bf16[2048,1024]{1,0:T(8,128)(2,1)}) %all-gather.3.cloned.1.call-update) | async-done | bytes 4194320 | tf_op jit(solution)/shard_map/all_gather | solution.py:83
  45.5 23.4 %fusion.2 = bf16[4096,1024]{1,0:T(8,128)(2,1)} fusion(bf16[2048,1024]{1,0:T(8,128)(2,1)} %all-gather.3.cloned.1.call-done, bf16[4096,1,2048]{2,0,1:T(8,128)(2,1)} %param.6), kind=kOutput, calls=%fused_computation.4 | convolution fusion | flops 17184063488 | bytes 29360128 | tf_op jit(solution)/shard_map/dot_general | solution.py:85
  69.0 9.7 copy.160
  78.6 8.1 copy.130
  88.8 7.4 gather_fusion.1
  96.3 2.7 copy_select_fusion
  99.0 3.9 all-to-all-start
  108.1 21.1 %all-to-all-done = bf16[8,8,128,128]{3,1,2,0:T(8,128)(2,1)S(1)} async-done(((bf16[8,8,128,128]{3,1,2,0:T(8,128)(2,1)}), bf16[8,8,128,128]{3,1,2,0:T(8,128)(2,1)S(1)}, u32[]{:S(2)}, u32[]{:S(2)}) %all-to-all-start) | async-done | bytes 2097184 | tf_op jit(solution)/shard_map/all_to_all | solution.py:58
  129.2 5.5 all-to-all-start.2
  136.3 3.1 copy.132
  139.3 33.0 %all-to-all-done.2 = bf16[8,128,1536]{2,1,0:T(8,128)(2,1)} async-done(((bf16[8,128,1536]{2,1,0:T(8,128)(2,1)}), bf16[8,128,1536]{2,1,0:T(8,128)(2,1)}, u32[]{:S(2)}, u32[]{:S(2)}) %all-to-all-start.2) | async-done | bytes 3145760 | tf_op jit(solution)/shard_map/all_to_all | solution.py:57
  172.3 6.7 all-to-all-start.1
  179.1 3.8 convolution_bitcast_fusion
  182.9 5.4 copy.155
  192.8 51.0 %all-to-all-done.1 = bf16[16,8,128,128]{3,2,1,0:T(8,128)(2,1)} async-done(((bf16[16,8,128,128]{3,2,1,0:T(8,128)(2,1)}), bf16[16,8,128,128]{3,2,1,0:T(8,128)(2,1)}, u32[]{:S(2)}, u32[]{:S(2)}) %all-to-all-start.1) | async-done | bytes 4194336 | tf_op jit(solution)/shard_map/all_to_all | solution.py:71
  243.8 5.8 all-to-all-start.4
  249.6 4.2 convolution_convert_fusion
  253.8 6.2 copy.137
  260.0 15.9 %all-to-all-done.4 = bf16[8,128,1024]{2,1,0:T(8,128)(2,1)S(1)} async-done(((bf16[8,128,1024]{2,1,0:T(8,128)(2,1)}), bf16[8,128,1024]{2,1,0:T(8,128)(2,1)S(1)}, u32[]{:S(2)}, u32[]{:S(2)}) %all-to-all-start.4) | async-done | bytes 2097184 | tf_op jit(solution)/shard_map/all_to_all | solution.py:95
  275.9 4.6 all-to-all-start.3
  282.3 4.3 copy.143
  286.6 90.7 %all-to-all-done.3 = bf16[16,128,1536]{2,1,0:T(8,128)(2,1)} async-done(((bf16[16,128,1536]{2,1,0:T(8,128)(2,1)}), bf16[16,128,1536]{2,1,0:T(8,128)(2,1)}, u32[]{:S(2)}, u32[]{:S(2)}) %all-to-all-start.3) | async-done | bytes 6291488 | tf_op jit(solution)/shard_map/all_to_all | solution.py:70
  377.2 5.2 all-to-all-start.5
  382.7 467.4 %reduce-scatter.7.cloned.1.call-done = f32[8,1024]{1,0:T(8,128)} async-done(((f32[1024,1024]{1,0:T(8,128)}), f32[8,1024]{1,0:T(8,128)}) %reduce-scatter.7.cloned.1.call-update) | async-done | bytes 32784 | tf_op jit(solution)/shard_map/reduce_scatter | solution.py:91
  851.8 4.6 fusion.20
  856.5 2.8 convolution_bitcast_fusion.1
  859.2 6.4 fusion.12
  870.0 2.9 fusion.26
  872.9 4.9 fusion.8
  877.8 4.4 copy.145
  882.2 68.5 %all-gather.5.cloned.1.call-done = bf16[1024,1024]{1,0:T(8,128)(2,1)} async-done(((bf16[8,1024]{1,0:T(8,128)(2,1)}), bf16[1024,1024]{1,0:T(8,128)(2,1)}) %all-gather.5.cloned.1.call-update) | async-done | bytes 2097168 | tf_op jit(solution)/shard_map/all_gather | solution.py:92
  950.7 5.8 fusion.7
  (66 shorter events, 26.4 us)
Async XLA Ops:
  7.2 849.3 %copy-start = (bf16[1,1,1024,512]{3,2,1,0:T(8,128)(2,1)S(1)}, bf16[1,1,1024,512]{3,2,1,0:T(8,128)(2,1)}, u32[]{:S(2)}) copy-start(bf16[1,1,1024,512]{3,2,1,0:T(8,128)(2,1)} %param.9) | copy-start | bytes 3145732
  7.2 38.3 %all-gather.3.cloned.1.call-start = ((), (), s32[]{:S(2)}) async-start(), calls=%async_computation.8 | async-start | bytes 4718592 | tf_op jit(solution)/shard_map/all_gather | solution.py:83
  7.9 171.2 %reduce-scatter.5.cloned.1.call-start = ((), (), s32[]{:S(2)}) async-start(), calls=%async_computation.9 | async-start | bytes 8912896 | tf_op jit(solution)/shard_map/reduce_scatter | solution.py:84
  78.6 8.2 copy-start.7
  78.6 8.3 copy-start.6
  99.0 4.1 copy-start.5
  99.0 30.3 %all-to-all-start = ((bf16[8,8,128,128]{3,1,2,0:T(8,128)(2,1)}), bf16[8,8,128,128]{3,1,2,0:T(8,128)(2,1)S(1)}, u32[]{:S(2)}, u32[]{:S(2)}) async-start(bf16[8,8,128,128]{3,1,2,0:T(8,128)(2,1)} %copy_select_fusion), calls=%async_computation | async-start | bytes 4194304 | tf_op jit(solution)/shard_map/all_to_all | solution.py:58
  129.2 43.1 %all-to-all-start.2 = ((bf16[8,128,1536]{2,1,0:T(8,128)(2,1)}), bf16[8,128,1536]{2,1,0:T(8,128)(2,1)}, u32[]{:S(2)}, u32[]{:S(2)}) async-start(bf16[8,128,1536]{2,1,0:T(8,128)(2,1)} %copy.135), calls=%async_computation.2 | async-start | bytes 6291456 | tf_op jit(solution)/shard_map/all_to_all | solution.py:57
  139.3 39.8 %copy-start.1 = (bf16[256,1024]{1,0:T(8,128)(2,1)S(1)}, bf16[256,1024]{1,0:T(8,128)(2,1)}, u32[]{:S(2)}) copy-start(bf16[256,1024]{1,0:T(8,128)(2,1)} %param.7) | copy-start | bytes 1572868
  172.3 71.5 %all-to-all-start.1 = ((bf16[16,8,128,128]{3,2,1,0:T(8,128)(2,1)}), bf16[16,8,128,128]{3,2,1,0:T(8,128)(2,1)}, u32[]{:S(2)}, u32[]{:S(2)}) async-start(bf16[16,8,128,128]{3,2,1,0:T(8,128)(2,1)} %copy.132), calls=%async_computation.1 | async-start | bytes 8388608 | tf_op jit(solution)/shard_map/all_to_all | solution.py:71
  179.0 671.0 %reduce-scatter.7.cloned.1.call-start = ((), (), s32[]{:S(2)}) async-start(), calls=%async_computation.11 | async-start | bytes 4227072 | tf_op jit(solution)/shard_map/reduce_scatter | solution.py:91
  188.2 1.0 copy-start.2
  243.8 32.1 %all-to-all-start.4 = ((bf16[8,128,1024]{2,1,0:T(8,128)(2,1)}), bf16[8,128,1024]{2,1,0:T(8,128)(2,1)S(1)}, u32[]{:S(2)}, u32[]{:S(2)}) async-start(bf16[8,128,1024]{2,1,0:T(8,128)(2,1)} %copy.141), calls=%async_computation.5 | async-start | bytes 4194304 | tf_op jit(solution)/shard_map/all_to_all | solution.py:95
  275.9 101.3 %all-to-all-start.3 = ((bf16[16,128,1536]{2,1,0:T(8,128)(2,1)}), bf16[16,128,1536]{2,1,0:T(8,128)(2,1)}, u32[]{:S(2)}, u32[]{:S(2)}) async-start(bf16[16,128,1536]{2,1,0:T(8,128)(2,1)} %copy.137), calls=%async_computation.3 | async-start | bytes 12582912 | tf_op jit(solution)/shard_map/all_to_all | solution.py:70
  377.2 495.7 %all-to-all-start.5 = ((bf16[16,128,1024]{2,1,0:T(8,128)(2,1)}), bf16[16,128,1024]{2,1,0:T(8,128)(2,1)}, u32[]{:S(2)}, u32[]{:S(2)}) async-start(bf16[16,128,1024]{2,1,0:T(8,128)(2,1)} %copy.143), calls=%async_computation.6 | async-start | bytes 8388608 | tf_op jit(solution)/shard_map/all_to_all | solution.py:97
  382.4 568.2 %all-gather.5.cloned.1.call-start = ((), (), s32[]{:S(2)}) async-start(), calls=%async_computation.10 | async-start | bytes 2113536 | tf_op jit(solution)/shard_map/all_gather | solution.py:92
  866.5 1.8 copy-start.3
  956.5 1.3 copy-start.4
Sparse Core Ops, SparseCore 0:
  9.7 35.7 all-gather.2
  69.1 83.4 reduce-scatter.4
  188.4 661.6 reduce-scatter.6
  853.3 97.3 all-gather.4
where the time goes:
time: 976 us; the launch traced here: 968 us
  waiting for transfers between devices  786 us (81%)
  matrix products  67.9 us (7%)
  local copies, waits for them, and re-layouts  61.3 us (6%)
  starting transfers between devices  32.1 us (3%)
  between operations  14.5 us (1%)
    reduce_scatter x1, waiting for transfers between devices, body(): lax.psum_scatter(occ_term, ('row', 'col'), scatter_dimension=0, tiled=True)  467 us
    all_to_all x1, waiting for transfers between devices, body(): lax.all_to_all(send2_rows, 'col', 0, 0, tiled=True)  90.7 us
    all_gather x1, waiting for transfers between devices, body(): lax.all_gather(occ_part.astype(BF16), ('row', 'col'), axis=0, tiled=True)  68.5 us
    all_to_all x1, waiting for transfers between devices, body(): lax.all_to_all(send2_fock, 'col', 0, 0, tiled=True)  51 us
    all_gather x1, waiting for transfers between devices, body(): gathered = lax.all_gather(lmo_coef, 'row', axis=0, tiled=True)  37.6 us
    all_to_all x1, waiting for transfers between devices, body(): lax.all_to_all(send1_rows, 'row', 0, 0, tiled=True)  33 us
    dot_general x1, matrix products, body(): jnp.dot(panel_fock, gathered, preferred_element_type=F32).astype(BF16)  23.4 us
    all_to_all x1, waiting for transfers between devices, body(): lax.all_to_all(send1_fock, 'row', 0, 0, tiled=True)  21.1 us
  transfers between devices with their start and end apart: 10, of which 8 were waited for; matrix products, arithmetic and copies ran while one was open for 10% of the time, Pallas kernels for 0%

commit v1 on v0

--- a/solution.py
+++ b/solution.py
@@ -6,6 +6,12 @@
 BLK = 128
 F32 = jnp.float32
 BF16 = jnp.bfloat16
+
+
+def tiled_gather(x, axis, dim):
+    devices = lax.axis_size(axis)
+    repeats = [devices if d == dim else 1 for d in range(x.ndim)]
+    return lax.all_to_all(jnp.tile(x, repeats), axis, split_axis=dim, concat_axis=dim, tiled=True)
 
 
 def pick(mask, table):
@@ -80,7 +86,7 @@
         BF16
     )
     domain_fock = domain_fock.reshape(dom_width, dom_width)
-    gathered = lax.all_gather(lmo_coef, "row", axis=0, tiled=True)
+    gathered = tiled_gather(lmo_coef, "row", 0)
     coef_b = lax.psum_scatter(
         jnp.dot(panel_fock, gathered, preferred_element_type=F32).astype(BF16),
         "col",

time: 976 us -> 996 us (1.020)
  blocking collectives: 0 us -> 55.1 us
  waiting for transfers between devices: 786 us -> 748 us
    all_to_all x0 -> x1, blocking collectives: none -> 55.1 us  [tiled_gather(): lax.all_to_all(jnp.tile(x, repeats), axis, split_axis=dim, concat_axis=di...]
    all_gather x1 -> x0, waiting for transfers between devices: 37.6 us -> none  [body(): gathered = lax.all_gather(lmo_coef, 'row', axis=0, tiled=True)]
  transfers between devices with their start and end apart: 10 -> 9, of which waited for: 8 -> 7; matrix products, arithmetic and copies ran while one was open for 10% -> 10% of each run, Pallas kernels for 0% -> 0%
where the time goes in v1:
time: 996 us; the launch traced here: 986 us
  waiting for transfers between devices  748 us (75%)
  matrix products  66.7 us (7%)
  local copies, waits for them, and re-layouts  62.9 us (6%)
  blocking collectives  55.1 us (6%)
  starting transfers between devices  33.6 us (3%)
  between operations  14.5 us (1%)
    reduce_scatter x1, waiting for transfers between devices, body(): lax.psum_scatter(occ_term, ('row', 'col'), scatter_dimension=0, tiled=True)  468 us
    all_to_all x1, waiting for transfers between devices, body(): lax.all_to_all(send2_rows, 'col', 0, 0, tiled=True)  90.7 us
    all_gather x1, waiting for transfers between devices, body(): lax.all_gather(occ_part.astype(BF16), ('row', 'col'), axis=0, tiled=True)  68.2 us
    all_to_all x1, blocking collectives, tiled_gather(): lax.all_to_all(jnp.tile(x, repeats), axis, split_axis=dim, concat_axis=di...  55.1 us
    all_to_all x1, waiting for transfers between devices, body(): lax.all_to_all(send2_fock, 'col', 0, 0, tiled=True)  51 us
    all_to_all x1, waiting for transfers between devices, body(): lax.all_to_all(send1_rows, 'row', 0, 0, tiled=True)  33 us
    dot_general x1, matrix products, body(): jnp.dot(panel_fock, gathered, preferred_element_type=F32).astype(BF16)  22.2 us
    all_to_all x1, waiting for transfers between devices, body(): lax.all_to_all(send1_fock, 'row', 0, 0, tiled=True)  21 us
  transfers between devices with their start and end apart: 9, of which 7 were waited for; matrix products, arithmetic and copies ran while one was open for 10% of the time, Pallas kernels for 0%

profile of v1, /device:TPU:1, one launch (start us, length us, event | category | flops | bytes accessed | tf_op | source)
XLA Modules:
  0.0 986.5 jit_solution(7304236132089039402)
XLA Ops:
  8.9 55.1 %all_to_all.39 = bf16[8,256,1024]{2,1,0:T(8,128)(2,1)S(1)} all-to-all(bf16[8,256,1024]{2,1,0:T(8,128)(2,1)S(1)} %tile.2), channel_id=1, replica_groups=mesh['row'=8,'col'=16] {'row'}, dimensions={0} | all-to-all | bytes 8388608 | tf_op jit(solution)/shard_map/all_to_all | solution.py:14
  63.9 22.2 %fusion.2 = bf16[4096,1024]{1,0:T(8,128)(2,1)} fusion(bf16[2048,1024]{1,0:T(8,128)(2,1)S(1)} %bitcast.136, bf16[4096,1,2048]{2,0,1:T(8,128)(2,1)} %param.6), kind=kOutput, calls=%fused_computation.4 | convolution fusion | flops 17184063488 | bytes 29360128 | tf_op jit(solution)/shard_map/dot_general | solution.py:91
  86.1 9.7 copy.160
  95.8 8.2 copy.130
  106.0 7.4 gather_fusion.1
  113.5 2.7 copy_select_fusion
  116.2 4.7 all-to-all-start
  126.2 21.0 %all-to-all-done = bf16[8,8,128,128]{3,1,2,0:T(8,128)(2,1)S(1)} async-done(((bf16[8,8,128,128]{3,1,2,0:T(8,128)(2,1)}), bf16[8,8,128,128]{3,1,2,0:T(8,128)(2,1)S(1)}, u32[]{:S(2)}, u32[]{:S(2)}) %all-to-all-start) | async-done | bytes 2097184 | tf_op jit(solution)/shard_map/all_to_all | solution.py:64
  147.2 5.5 all-to-all-start.2
  154.3 3.1 copy.132
  157.3 33.0 %all-to-all-done.2 = bf16[8,128,1536]{2,1,0:T(8,128)(2,1)} async-done(((bf16[8,128,1536]{2,1,0:T(8,128)(2,1)}), bf16[8,128,1536]{2,1,0:T(8,128)(2,1)}, u32[]{:S(2)}, u32[]{:S(2)}) %all-to-all-start.2) | async-done | bytes 3145760 | tf_op jit(solution)/shard_map/all_to_all | solution.py:63
  190.3 7.6 all-to-all-start.1
  198.0 3.8 convolution_bitcast_fusion
  201.8 5.4 copy.155
  211.8 51.0 %all-to-all-done.1 = bf16[16,8,128,128]{3,2,1,0:T(8,128)(2,1)} async-done(((bf16[16,8,128,128]{3,2,1,0:T(8,128)(2,1)}), bf16[16,8,128,128]{3,2,1,0:T(8,128)(2,1)}, u32[]{:S(2)}, u32[]{:S(2)}) %all-to-all-start.1) | async-done | bytes 4194336 | tf_op jit(solution)/shard_map/all_to_all | solution.py:77
  262.7 5.8 all-to-all-start.5
  268.5 4.2 convolution_convert_fusion
  272.8 6.1 copy.137
  278.9 16.0 %all-to-all-done.5 = bf16[8,128,1024]{2,1,0:T(8,128)(2,1)S(1)} async-done(((bf16[8,128,1024]{2,1,0:T(8,128)(2,1)}), bf16[8,128,1024]{2,1,0:T(8,128)(2,1)S(1)}, u32[]{:S(2)}, u32[]{:S(2)}) %all-to-all-start.5) | async-done | bytes 2097184 | tf_op jit(solution)/shard_map/all_to_all | solution.py:101
  294.9 4.6 all-to-all-start.3
  301.2 4.3 copy.143
  305.5 90.7 %all-to-all-done.3 = bf16[16,128,1536]{2,1,0:T(8,128)(2,1)} async-done(((bf16[16,128,1536]{2,1,0:T(8,128)(2,1)}), bf16[16,128,1536]{2,1,0:T(8,128)(2,1)}, u32[]{:S(2)}, u32[]{:S(2)}) %all-to-all-start.3) | async-done | bytes 6291488 | tf_op jit(solution)/shard_map/all_to_all | solution.py:76
  396.2 5.1 all-to-all-start.6
  401.6 467.6 %reduce-scatter.7.cloned.1.call-done = f32[8,1024]{1,0:T(8,128)} async-done(((f32[1024,1024]{1,0:T(8,128)}), f32[8,1024]{1,0:T(8,128)}) %reduce-scatter.7.cloned.1.call-update) | async-done | bytes 32784 | tf_op jit(solution)/shard_map/reduce_scatter | solution.py:97
  871.0 4.6 fusion.20
  875.6 2.8 convolution_bitcast_fusion.1
  878.4 6.4 fusion.12
  889.1 2.9 fusion.26
  892.0 4.9 fusion.8
  896.9 4.4 copy.145
  901.3 68.2 %all-gather.2.cloned.1.call-done = bf16[1024,1024]{1,0:T(8,128)(2,1)} async-done(((bf16[8,1024]{1,0:T(8,128)(2,1)}), bf16[1024,1024]{1,0:T(8,128)(2,1)}) %all-gather.2.cloned.1.call-update) | async-done | bytes 2097168 | tf_op jit(solution)/shard_map/all_gather | solution.py:98
  969.5 5.8 fusion.7
  (65 shorter events, 27.4 us)
Async XLA Ops:
  7.2 868.4 %copy-start = (bf16[1,1,1024,512]{3,2,1,0:T(8,128)(2,1)S(1)}, bf16[1,1,1024,512]{3,2,1,0:T(8,128)(2,1)}, u32[]{:S(2)}) copy-start(bf16[1,1,1024,512]{3,2,1,0:T(8,128)(2,1)} %param.9) | copy-start | bytes 3145732
  7.2 190.8 %reduce-scatter.5.cloned.1.call-start = ((), (), s32[]{:S(2)}) async-start(), calls=%async_computation.9 | async-start | bytes 8912896 | tf_op jit(solution)/shard_map/reduce_scatter | solution.py:90
  95.8 8.2 copy-start.7
  95.8 8.3 copy-start.6
  116.2 4.8 copy-start.5
  116.2 31.0 %all-to-all-start = ((bf16[8,8,128,128]{3,1,2,0:T(8,128)(2,1)}), bf16[8,8,128,128]{3,1,2,0:T(8,128)(2,1)S(1)}, u32[]{:S(2)}, u32[]{:S(2)}) async-start(bf16[8,8,128,128]{3,1,2,0:T(8,128)(2,1)} %copy_select_fusion), calls=%async_computation | async-start | bytes 4194304 | tf_op jit(solution)/shard_map/all_to_all | solution.py:64
  147.2 43.1 %all-to-all-start.2 = ((bf16[8,128,1536]{2,1,0:T(8,128)(2,1)}), bf16[8,128,1536]{2,1,0:T(8,128)(2,1)}, u32[]{:S(2)}, u32[]{:S(2)}) async-start(bf16[8,128,1536]{2,1,0:T(8,128)(2,1)} %copy.135), calls=%async_computation.2 | async-start | bytes 6291456 | tf_op jit(solution)/shard_map/all_to_all | solution.py:63
  157.3 40.7 %copy-start.1 = (bf16[256,1024]{1,0:T(8,128)(2,1)S(1)}, bf16[256,1024]{1,0:T(8,128)(2,1)}, u32[]{:S(2)}) copy-start(bf16[256,1024]{1,0:T(8,128)(2,1)} %param.7) | copy-start | bytes 1572868
  190.3 72.4 %all-to-all-start.1 = ((bf16[16,8,128,128]{3,2,1,0:T(8,128)(2,1)}), bf16[16,8,128,128]{3,2,1,0:T(8,128)(2,1)}, u32[]{:S(2)}, u32[]{:S(2)}) async-start(bf16[16,8,128,128]{3,2,1,0:T(8,128)(2,1)} %copy.132), calls=%async_computation.1 | async-start | bytes 8388608 | tf_op jit(solution)/shard_map/all_to_all | solution.py:77
  198.0 671.2 %reduce-scatter.7.cloned.1.call-start = ((), (), s32[]{:S(2)}) async-start(), calls=%async_computation.11 | async-start | bytes 4227072 | tf_op jit(solution)/shard_map/reduce_scatter | solution.py:97
  207.2 1.0 copy-start.2
  262.7 32.2 %all-to-all-start.5 = ((bf16[8,128,1024]{2,1,0:T(8,128)(2,1)}), bf16[8,128,1024]{2,1,0:T(8,128)(2,1)S(1)}, u32[]{:S(2)}, u32[]{:S(2)}) async-start(bf16[8,128,1024]{2,1,0:T(8,128)(2,1)} %copy.141), calls=%async_computation.6 | async-start | bytes 4194304 | tf_op jit(solution)/shard_map/all_to_all | solution.py:101
  294.9 101.4 %all-to-all-start.3 = ((bf16[16,128,1536]{2,1,0:T(8,128)(2,1)}), bf16[16,128,1536]{2,1,0:T(8,128)(2,1)}, u32[]{:S(2)}, u32[]{:S(2)}) async-start(bf16[16,128,1536]{2,1,0:T(8,128)(2,1)} %copy.137), calls=%async_computation.3 | async-start | bytes 12582912 | tf_op jit(solution)/shard_map/all_to_all | solution.py:76
  396.2 495.8 %all-to-all-start.6 = ((bf16[16,128,1024]{2,1,0:T(8,128)(2,1)}), bf16[16,128,1024]{2,1,0:T(8,128)(2,1)}, u32[]{:S(2)}, u32[]{:S(2)}) async-start(bf16[16,128,1024]{2,1,0:T(8,128)(2,1)} %copy.143), calls=%async_computation.7 | async-start | bytes 8388608 | tf_op jit(solution)/shard_map/all_to_all | solution.py:103
  401.3 568.2 %all-gather.2.cloned.1.call-start = ((), (), s32[]{:S(2)}) async-start(), calls=%async_computation.10 | async-start | bytes 2113536 | tf_op jit(solution)/shard_map/all_gather | solution.py:98
  885.7 1.7 copy-start.3
  975.3 1.3 copy-start.4
Sparse Core Ops, SparseCore 0:
  86.3 84.7 reduce-scatter.4
  207.3 661.8 reduce-scatter.6
  872.6 96.8 all-gather.1
